TPU v7x, 512 devices: a whole 4x8x8 slice. The times are simulated.
512 devices in a mesh: inp: 64 (over y_lo, z, x), tm: 8 (over y_hi, core).
Axes of the slice: x: 4, y: 8 (y_hi: 4, y_lo: 2; y = y_hi * 2 + y_lo), z: 8, core: 2. Of those that a mesh axis runs over, the one named last changes fastest.
Arguments:
- samples: bfloat16 [1024, 64, 1024], P('inp', 'tm'), may hold values from -8 to 8
- filter_taps: float32 [4, 1024], replicated, may hold values from -0.09375 to 0.09375
- partner_mask: int32 [2], replicated, may hold values from 1 to 63, as said below
Outputs:
- visibilities: float32 [1024, 3, 16, 1024], P('inp', None, None, 'tm')
Inputs may be any that keep to these rules, and one draw needn't show every extreme that they name: `partner_mask`: the 2 masks are distinct and one of them is 63; in a round, input block p pairs with input block p XOR the mask.
All inputs are finite; a program needn't handle non-finite values.
Results may differ from a plain program's by a relative error of at most 0.0009.
Values may be sent and summed in bfloat16 or wider, within the bound.
No kernel may reach another device: no remote copies, remote signals or barrier semaphores. Data moves between devices by JAX's collectives and lax.ppermute only.
A program may use at most 64 MiB of HBM per device.

v0:
```python
import math

import jax
import jax.numpy as jnp
from jax import lax
from jax.sharding import PartitionSpec as P

TAPS = 4
ROUNDS = 2


def shifted(block, axis, distance):
    devices = range(lax.axis_size(axis))
    route = [(i - distance, i) for i in devices if i - distance in devices]
    return lax.ppermute(block, axis, route)


def dft_columns(n_fft):
    channels = n_fft // 2
    sample_ids = jnp.arange(n_fft, dtype=jnp.int32)[:, None]
    chan_ids = jnp.arange(channels, dtype=jnp.int32)[None, :]
    phase = (sample_ids * chan_ids % n_fft).astype(jnp.float32) * (2.0 * math.pi / n_fft)
    return jnp.concatenate([jnp.cos(phase), -jnp.sin(phase)], axis=1)


def channelize(samples, filter_taps):
    in_dev, spec_dev, n_fft = samples.shape
    history = shifted(samples[:, spec_dev - (TAPS - 1) :, :], "tm", 1)
    frames = jnp.concatenate([history, samples], axis=1)
    filtered = jnp.zeros((in_dev, spec_dev, n_fft), jnp.float32)
    for tap_index in range(TAPS):
        filtered = filtered + filter_taps[tap_index][None, None, :] * frames[
            :, tap_index : tap_index + spec_dev, :
        ].astype(jnp.float32)
    dft_table = dft_columns(n_fft)
    spectra = jnp.dot(
        filtered.reshape(in_dev * spec_dev, n_fft),
        dft_table,
        precision=lax.Precision.HIGHEST,
        preferred_element_type=jnp.float32,
    )
    return spectra.astype(jnp.bfloat16).reshape(in_dev, spec_dev, 2, n_fft // 2)


def by_channel_chunk(block, tm_size):
    in_dev, spec_dev, both_parts, channels = block.shape
    chunks = tm_size // both_parts
    width = channels // chunks
    grouped = block.reshape(in_dev, spec_dev, both_parts, chunks, width)
    grouped = jnp.transpose(grouped, (3, 0, 1, 2, 4))
    send = jnp.concatenate([grouped] * (tm_size // chunks), axis=0)
    got = lax.all_to_all(send, "tm", 0, 0, tiled=True)
    got = jnp.transpose(got, (1, 0, 2, 3, 4))
    return got.reshape(in_dev, tm_size * spec_dev, both_parts, width)


def column_terms(left, right, imag_half):
    left_re = left[:, :, 0, :].astype(jnp.float32)
    left_im = left[:, :, 1, :].astype(jnp.float32)
    first = jnp.where(imag_half, left_im, left_re)
    second = jnp.where(imag_half, -left_re, left_im)
    right_re = right[None, :, :, 0, :].astype(jnp.float32)
    right_im = right[None, :, :, 1, :].astype(jnp.float32)
    return jnp.sum(first[:, None] * right_re + second[:, None] * right_im, axis=2)


def on_device(samples, filter_taps, partner_mask):
    spectra = channelize(samples, filter_taps)
    tm_size = lax.axis_size("tm")
    own_block = by_channel_chunk(spectra, tm_size)
    norm_scale = 1.0 / own_block.shape[1]
    inp_size = lax.axis_size("inp")
    all_bits = inp_size - 1
    imag_half = lax.axis_index("tm") >= tm_size // 2

    def exchange(m):
        def both(x):
            full = lax.ppermute(x, "inp", [(i, i ^ all_bits) for i in range(inp_size)])
            other = lax.ppermute(x, "inp", [(i, i ^ m) for i in range(inp_size)])
            return full, other
        return both

    other_mask = jnp.where(partner_mask[0] == all_bits, partner_mask[1], partner_mask[0])
    branches = [exchange(m) for m in range(1, all_bits)]
    full_partner, other_partner = lax.switch(
        jnp.clip(other_mask - 1, 0, all_bits - 2), branches, own_block
    )
    pair_terms = [column_terms(own_block, own_block, imag_half)]
    for round_index in range(ROUNDS):
        is_full = partner_mask[round_index] == all_bits
        partner = jnp.where(is_full, full_partner, other_partner)
        pair_terms.append(column_terms(own_block, partner, imag_half))
    return jnp.stack(pair_terms, axis=1) * norm_scale


def solution(mesh):
    in_specs = (P("inp", "tm", None), P(), P())
    out_specs = P("inp", None, None, "tm")
    return jax.shard_map(
        on_device, mesh=mesh, in_specs=in_specs, out_specs=out_specs, check_vma=False
    )
```

profile of v0, /device:TPU:64, one launch (start us, length us, event | category | flops | bytes accessed | tf_op | source)
XLA Modules:
  0.0 106.0 jit_solution(1691717658401822918)
XLA Ops:
  0.0 1.0 slice.58
  1.0 0.0 copy-start.1
  1.0 0.0 copy-start
  1.0 1.9 %collective-permute-start.124 = (bf16[16,3,1024]{2,1,0:T(4,128)(2,1)S(1)}, bf16[16,3,1024]{2,1,0:T(4,128)(2,1)S(1)}, u32[]{:S(2)}, u32[]{:S(2)}) collective-permute-start(bf16[16,3,1024]{2,1,0:T(4,128)(2,1)S(1)} %slice.58), channel_id=1, source_target_pairs={{0,1},{1,2},{2,3},{3,4},{4,5},{5,6},{6,7},{8,9},{9,10},{10,11},{11... | collective-permute-start | bytes 294920 | tf_op jit(solution)/shard_map/ppermute | solution.py:15
  2.9 8.2 %sine_negate_fusion = (f32[1024,512]{1,0:T(8,128)S(1)}, f32[1024,512]{1,0:T(8,128)S(1)}) fusion(), kind=kLoop, calls=%fused_computation.13 | loop fusion | flops 7864320 | bytes 4194304 | tf_op jit(solution)/shard_map/neg | solution.py:23
  11.2 2.7 %fusion.10 = bf16[128,1024]{1,0:T(8,128)(2,1)S(1)} fusion(f32[1024,512]{1,0:T(8,128)S(1)} %get-tuple-element.90, f32[1024,512]{1,0:T(8,128)S(1)} %get-tuple-element.91, bf16[16,8,1024]{2,1,0:T(8,128)(2,1)S(1)} %copy-done, bf16[16,3,1024]{2,1,0:T(4,128)(2,1)S(1)} %collective-permute-done.124, f32[1024]{0:T(1024)S(1)} %bitcast.65, f32[1024]{0:T(1024)S(1)} %bitcast.66, ...), kind=kOutput, calls=%fused_computation.17 | convolution fusion | flops 1614413824 | bytes 4833280 | tf_op jit(solution)/shard_map/dot_general | solution.py:36
  14.0 0.0 copy-start.2
  14.0 0.8 pad_maximum_fusion
  14.9 7.8 %all-to-all-start = ((bf16[8,16,8,2,128]{4,2,3,1,0:T(8,128)(2,1)}), bf16[8,16,8,2,128]{4,2,3,1,0:T(8,128)(2,1)S(1)}, u32[]{:S(2)}, u32[]{:S(2)}) async-start(bf16[8,16,8,2,128]{4,2,3,1,0:T(8,128)(2,1)} %pad_maximum_fusion), calls=%async_computation | async-start | bytes 1048576 | tf_op jit(solution)/shard_map/all_to_all | solution.py:52
  22.7 0.6 fusion.40
  25.9 14.4 %all-to-all-done = bf16[8,16,8,2,128]{4,2,3,1,0:T(8,128)(2,1)S(1)} async-done(((bf16[8,16,8,2,128]{4,2,3,1,0:T(8,128)(2,1)}), bf16[8,16,8,2,128]{4,2,3,1,0:T(8,128)(2,1)S(1)}, u32[]{:S(2)}, u32[]{:S(2)}) %all-to-all-start) | async-done | bytes 524320 | tf_op jit(solution)/shard_map/all_to_all | solution.py:52
  40.4 0.1 copy.142
  40.5 0.5 copy.76
  41.1 0.1 fusion.30
  41.2 54.1 %conditional.1 = (bf16[16,64,2,128]{3,2,1,0:T(2,128)(2,1)}, bf16[16,64,2,128]{3,2,1,0:T(2,128)(2,1)}) conditional(s32[]{:T(128)} %clamp.3, bf16[16,64,2,128]{3,2,1,0:T(2,128)(2,1)S(1)} %copy.76, bf16[16,64,2,128]{3,2,1,0:T(2,128)(2,1)S(1)} %copy.76, bf16[16,64,2,128]{3,2,1,0:T(2,128)(2,1)S(1)} %copy.76, ...), branch_computations={%region_1.2_spmd, %region_2.3_spmd, %region_3.4_spmd, %region_4.5_... | conditional | bytes 4194400 | solution.py:85
  41.2 10.0 %collective-permute-start.31 = (bf16[16,64,2,128]{3,2,1,0:T(2,128)(2,1)S(1)}, bf16[16,64,2,128]{3,2,1,0:T(2,128)(2,1)}, u32[]{:S(2)}, u32[]{:S(2)}) collective-permute-start(bf16[16,64,2,128]{3,2,1,0:T(2,128)(2,1)S(1)} %param.15), channel_id=1, source_target_pairs={{0,128},{8,136},{16,144},{24,152},{32,160},{40,168},{48,176},{56,1... | collective-permute-start | bytes 1572872 | tf_op jit(solution)/shard_map/cond/branch_15_fun/ppermute | solution.py:79
  51.2 3.1 %collective-permute-start.30 = (bf16[16,64,2,128]{3,2,1,0:T(2,128)(2,1)S(1)}, bf16[16,64,2,128]{3,2,1,0:T(2,128)(2,1)}, u32[]{:S(2)}, u32[]{:S(2)}) collective-permute-start(bf16[16,64,2,128]{3,2,1,0:T(2,128)(2,1)S(1)} %param.15), channel_id=1, source_target_pairs={{0,504},{8,496},{16,488},{24,480},{32,472},{40,464},{48,456},{56,4... | collective-permute-start | bytes 1572872 | tf_op jit(solution)/shard_map/cond/branch_15_fun/ppermute | solution.py:78
  54.4 40.9 %collective-permute-done.31 = bf16[16,64,2,128]{3,2,1,0:T(2,128)(2,1)} collective-permute-done((bf16[16,64,2,128]{3,2,1,0:T(2,128)(2,1)S(1)}, bf16[16,64,2,128]{3,2,1,0:T(2,128)(2,1)}, u32[]{:S(2)}, u32[]{:S(2)}) %collective-permute-start.31) | collective-permute-done | bytes 524320 | tf_op jit(solution)/shard_map/cond/branch_15_fun/ppermute | solution.py:79
  95.3 1.3 %broadcast_select_fusion = (bf16[16,16,8,128]{3,2,1,0:T(8,128)(2,1)S(1)}, bf16[16,16,8,128]{3,2,1,0:T(8,128)(2,1)S(1)}) fusion(bf16[16,16,8,128]{3,2,1,0:T(8,128)(2,1)} %bitcast.45, bf16[16,16,8,128]{3,2,1,0:T(8,128)(2,1)} %bitcast.46, pred[]{:T(512)S(6)} %eq.10, pred[]{:T(512)S(6)} %eq.9), kind=kLoop, calls=%fused_computation.19 | loop fusion | flops 524288 | bytes 2097154 | tf_op jit(solution)/shard_map/jit(_where)/select_n | solution.py:91
  96.6 1.1 %slice_convert_fusion.1 = (f32[16,64,1,128]{3,2,1,0:T(1,128)S(1)}, f32[16,64,1,128]{3,2,1,0:T(1,128)S(1)}) fusion(bf16[16,64,2,128]{3,2,1,0:T(2,128)(2,1)S(1)} %bitcast.53), kind=kLoop, calls=%fused_computation.26 | loop fusion | flops 262144 | bytes 1572864 | tf_op jit(solution)/shard_map/convert_element_type | solution.py:62
  97.7 1.1 %slice_convert_fusion.3 = (f32[16,64,1,128]{3,2,1,0:T(1,128)S(1)}, f32[16,64,1,128]{3,2,1,0:T(1,128)S(1)}) fusion(bf16[16,64,2,128]{3,2,1,0:T(2,128)(2,1)S(1)} %bitcast.52), kind=kLoop, calls=%fused_computation.28 | loop fusion | flops 262144 | bytes 1572864 | tf_op jit(solution)/shard_map/convert_element_type | solution.py:62
  98.7 0.1 broadcast_select_fusion.2
  98.9 6.3 %add_reduce_fusion.2 = (f32[16,16,128]{2,1,0:T(8,128)S(1)}, f32[16,16,128]{2,1,0:T(8,128)S(1)}, f32[16,16,128]{2,1,0:T(8,128)S(1)}) fusion(f32[16,64,128]{2,1,0:T(8,128)S(1)} %get-tuple-element.83, f32[16,64,128]{2,1,0:T(8,128)S(1)} %get-tuple-element.81, f32[16,64,128]{2,1,0:T(8,128)S(1)} %get-tuple-element.82, f32[16,64,128]{2,1,0:T(8,128)S(1)} %get-tuple-element.80, ...), kind=kLoop, calls=%fused_computation.2 | loop fusion | flops 25067520 | bytes 4587520 | tf_op jit(solution)/shard_map/reduce_sum | solution.py:64
  105.3 0.8 copy.138
  (8 shorter events, 0.1 us)
Async XLA Ops:
  1.0 10.2 %copy-start.1 = (f32[4,1024]{1,0:T(4,128)S(1)}, f32[4,1024]{1,0:T(4,128)}, u32[]{:S(2)}) copy-start(f32[4,1024]{1,0:T(4,128)} %param.66) | copy-start | bytes 49156
  1.0 10.2 %copy-start = (bf16[16,8,1024]{2,1,0:T(8,128)(2,1)S(1)}, bf16[16,8,1024]{2,1,0:T(8,128)(2,1)}, u32[]{:S(2)}) copy-start(bf16[16,8,1024]{2,1,0:T(8,128)(2,1)} %param.65) | copy-start | bytes 786436
  1.0 10.2 %collective-permute-start.124 = (bf16[16,3,1024]{2,1,0:T(4,128)(2,1)S(1)}, bf16[16,3,1024]{2,1,0:T(4,128)(2,1)S(1)}, u32[]{:S(2)}, u32[]{:S(2)}) collective-permute-start(bf16[16,3,1024]{2,1,0:T(4,128)(2,1)S(1)} %slice.58), channel_id=1, source_target_pairs={{0,1},{1,2},{2,3},{3,4},{4,5},{5,6},{6,7},{8,9},{9,10},{10,11},{11... | collective-permute-start | bytes 294920 | tf_op jit(solution)/shard_map/ppermute | solution.py:15
  14.0 8.7 %copy-start.2 = (s32[2]{0:T(128)S(1)}, s32[2]{0:T(128)}, u32[]{:S(2)}) copy-start(s32[2]{0:T(128)} %param.67) | copy-start | bytes 28
  14.9 25.5 %all-to-all-start = ((bf16[8,16,8,2,128]{4,2,3,1,0:T(8,128)(2,1)}), bf16[8,16,8,2,128]{4,2,3,1,0:T(8,128)(2,1)S(1)}, u32[]{:S(2)}, u32[]{:S(2)}) async-start(bf16[8,16,8,2,128]{4,2,3,1,0:T(8,128)(2,1)} %pad_maximum_fusion), calls=%async_computation | async-start | bytes 1048576 | tf_op jit(solution)/shard_map/all_to_all | solution.py:52
  41.2 54.1 %collective-permute-start.31 = (bf16[16,64,2,128]{3,2,1,0:T(2,128)(2,1)S(1)}, bf16[16,64,2,128]{3,2,1,0:T(2,128)(2,1)}, u32[]{:S(2)}, u32[]{:S(2)}) collective-permute-start(bf16[16,64,2,128]{3,2,1,0:T(2,128)(2,1)S(1)} %param.15), channel_id=1, source_target_pairs={{0,128},{8,136},{16,144},{24,152},{32,160},{40,168},{48,176},{56,1... | collective-permute-start | bytes 1572872 | tf_op jit(solution)/shard_map/cond/branch_15_fun/ppermute | solution.py:79
  51.2 44.1 %collective-permute-start.30 = (bf16[16,64,2,128]{3,2,1,0:T(2,128)(2,1)S(1)}, bf16[16,64,2,128]{3,2,1,0:T(2,128)(2,1)}, u32[]{:S(2)}, u32[]{:S(2)}) collective-permute-start(bf16[16,64,2,128]{3,2,1,0:T(2,128)(2,1)S(1)} %param.15), channel_id=1, source_target_pairs={{0,504},{8,496},{16,488},{24,480},{32,472},{40,464},{48,456},{56,4... | collective-permute-start | bytes 1572872 | tf_op jit(solution)/shard_map/cond/branch_15_fun/ppermute | solution.py:78
where the time goes:
time: 106 us
  waiting for transfers between devices  55.4 us (52%)
  starting transfers between devices  22.8 us (22%)
  other arithmetic  19.1 us (18%)
  local copies, waits for them, and re-layouts  3.14 us (3%)
  between operations  2.85 us (3%)
  matrix products  2.74 us (3%)
    ppermute x1, waiting for transfers between devices, both(): other = lax.ppermute(x, 'inp', [(i, i ^ m) for i in range(inp_size)])  40.9 us
    all_to_all x1, waiting for transfers between devices, by_channel_chunk(): got = lax.all_to_all(send, 'tm', 0, 0, tiled=True)  14.4 us
    ppermute x1, starting transfers between devices, both(): other = lax.ppermute(x, 'inp', [(i, i ^ m) for i in range(inp_size)])  10 us
    neg x1, other arithmetic, dft_columns(): return jnp.concatenate([jnp.cos(phase), -jnp.sin(phase)], axis=1)  8.24 us
    all_to_all x1, starting transfers between devices, by_channel_chunk(): got = lax.all_to_all(send, 'tm', 0, 0, tiled=True)  7.78 us
    reduce_sum x1, other arithmetic, column_terms(): jnp.sum(first[:, None] * right_re + second[:, None] * right_im, axis=2)  6.35 us
    ppermute x1, starting transfers between devices, both(): full = lax.ppermute(x, 'inp', [(i, i ^ all_bits) for i in range(inp_size)])  3.11 us
    dot_general x1, matrix products, channelize(): jnp.dot(filtered.reshape(in_dev * spec_dev, n_fft), dft_table, precision=...  2.74 us
  transfers between devices with their start and end apart: 4, of which 2 were waited for; matrix products, arithmetic and copies ran while one was open for 8% of the time, Pallas kernels for 0%

commit v1 on v0

--- a/solution.py
+++ b/solution.py
@@ -17,10 +17,19 @@
 
 def dft_columns(n_fft):
     channels = n_fft // 2
-    sample_ids = jnp.arange(n_fft, dtype=jnp.int32)[:, None]
+    coarse = int(round(math.sqrt(n_fft)))
+    fine = n_fft // coarse
     chan_ids = jnp.arange(channels, dtype=jnp.int32)[None, :]
-    phase = (sample_ids * chan_ids % n_fft).astype(jnp.float32) * (2.0 * math.pi / n_fft)
-    return jnp.concatenate([jnp.cos(phase), -jnp.sin(phase)], axis=1)
+    coarse_ids = jnp.arange(coarse, dtype=jnp.int32)[:, None]
+    fine_ids = jnp.arange(fine, dtype=jnp.int32)[:, None]
+    step = 2.0 * math.pi / n_fft
+    coarse_phase = (fine * coarse_ids * chan_ids % n_fft).astype(jnp.float32) * step
+    fine_phase = (fine_ids * chan_ids % n_fft).astype(jnp.float32) * step
+    cos_a, sin_a = jnp.cos(coarse_phase)[:, None], jnp.sin(coarse_phase)[:, None]
+    cos_b, sin_b = jnp.cos(fine_phase)[None], jnp.sin(fine_phase)[None]
+    cos_ab = (cos_a * cos_b - sin_a * sin_b).reshape(n_fft, channels)
+    sin_ab = (sin_a * cos_b + cos_a * sin_b).reshape(n_fft, channels)
+    return jnp.concatenate([cos_ab, -sin_ab], axis=1)
 
 
 def channelize(samples, filter_taps):

time: 106 us -> 88.8 us (0.84)
  the two profiles are of different devices: /device:TPU:64 before, /device:TPU:80 now
where the time goes in v1:
time: 88.8 us; the launch traced here: 88.5 us
  waiting for transfers between devices  45.1 us (51%)
  starting transfers between devices  22.6 us (25%)
  other arithmetic  12.1 us (14%)
  local copies, waits for them, and re-layouts  3.21 us (4%)
  matrix products  2.74 us (3%)
  between operations  2.72 us (3%)
    ppermute x1, waiting for transfers between devices, both(): other = lax.ppermute(x, 'inp', [(i, i ^ m) for i in range(inp_size)])  25.4 us
    all_to_all x1, waiting for transfers between devices, by_channel_chunk(): got = lax.all_to_all(send, 'tm', 0, 0, tiled=True)  12.6 us
    all_to_all x1, starting transfers between devices, by_channel_chunk(): got = lax.all_to_all(send, 'tm', 0, 0, tiled=True)  9.85 us
    ppermute x1, starting transfers between devices, both(): other = lax.ppermute(x, 'inp', [(i, i ^ m) for i in range(inp_size)])  8.29 us
    reduce_sum x1, other arithmetic, column_terms(): jnp.sum(first[:, None] * right_re + second[:, None] * right_im, axis=2)  6.35 us
    ppermute x1, waiting for transfers between devices, shifted(): return lax.ppermute(block, axis, route)  3.99 us
    ppermute x1, waiting for transfers between devices, both(): full = lax.ppermute(x, 'inp', [(i, i ^ all_bits) for i in range(inp_size)])  3.09 us
    dot_general x1, matrix products, channelize(): jnp.dot(filtered.reshape(in_dev * spec_dev, n_fft), dft_table, precision=...  2.74 us
  transfers between devices with their start and end apart: 4, of which 4 were waited for; matrix products, arithmetic and copies ran while one was open for 2% of the time, Pallas kernels for 0%

profile of v1, /device:TPU:80, one launch (start us, length us, event | category | flops | bytes accessed | tf_op | source)
XLA Modules:
  0.0 88.5 jit_solution(1308307706664971980)
XLA Ops:
  0.0 1.0 %slice.58 = bf16[16,3,1024]{2,1,0:T(4,128)(2,1)S(1)} slice(bf16[16,8,1024]{2,1,0:T(8,128)(2,1)} %param.65), slice={[0:16], [5:8], [0:1024]} | slice | bytes 196608 | tf_op jit(solution)/shard_map/slice | solution.py:37
  1.0 1.9 %collective-permute-start.124 = (bf16[16,3,1024]{2,1,0:T(4,128)(2,1)S(1)}, bf16[16,3,1024]{2,1,0:T(4,128)(2,1)S(1)}, u32[]{:S(2)}, u32[]{:S(2)}) collective-permute-start(bf16[16,3,1024]{2,1,0:T(4,128)(2,1)S(1)} %slice.58), channel_id=1, source_target_pairs={{0,1},{1,2},{2,3},{3,4},{4,5},{5,6},{6,7},{8,9},{9,10},{10,11},{11... | collective-permute-start | bytes 294920 | tf_op jit(solution)/shard_map/ppermute | solution.py:15
  3.0 0.3 fusion.42
  3.2 0.3 fusion.45
  3.6 0.6 multiply_subtract_fusion
  4.3 4.0 %collective-permute-done.124 = bf16[16,3,1024]{2,1,0:T(4,128)(2,1)S(1)} collective-permute-done((bf16[16,3,1024]{2,1,0:T(4,128)(2,1)S(1)}, bf16[16,3,1024]{2,1,0:T(4,128)(2,1)S(1)}, u32[]{:S(2)}, u32[]{:S(2)}) %collective-permute-start.124) | collective-permute-done | bytes 98336 | tf_op jit(solution)/shard_map/ppermute | solution.py:15
  8.3 2.7 %fusion.4 = bf16[128,1024]{1,0:T(8,128)(2,1)S(1)} fusion(f32[1024,512]{1,0:T(8,128)S(1)} %bitcast.57, f32[1024,512]{1,0:T(8,128)S(1)} %bitcast.56, bf16[16,8,1024]{2,1,0:T(8,128)(2,1)S(1)} %copy-done, bf16[16,3,1024]{2,1,0:T(4,128)(2,1)S(1)} %collective-permute-done.124, f32[1024]{0:T(1024)S(1)} %bitcast.69, f32[1024]{0:T(1024)S(1)} %bitcast.70, ...), kind=kOutput, calls=%fused_computation.9 | convolution fusion | flops 1614413824 | bytes 4833280 | tf_op jit(solution)/shard_map/dot_general | solution.py:45
  11.1 0.8 pad_maximum_fusion
  11.9 9.9 %all-to-all-start = ((bf16[8,16,8,2,128]{4,2,3,1,0:T(8,128)(2,1)}), bf16[8,16,8,2,128]{4,2,3,1,0:T(8,128)(2,1)S(1)}, u32[]{:S(2)}, u32[]{:S(2)}) async-start(bf16[8,16,8,2,128]{4,2,3,1,0:T(8,128)(2,1)} %pad_maximum_fusion), calls=%async_computation | async-start | bytes 1048576 | tf_op jit(solution)/shard_map/all_to_all | solution.py:61
  21.8 0.6 fusion.49
  25.0 12.6 %all-to-all-done = bf16[8,16,8,2,128]{4,2,3,1,0:T(8,128)(2,1)S(1)} async-done(((bf16[8,16,8,2,128]{4,2,3,1,0:T(8,128)(2,1)}), bf16[8,16,8,2,128]{4,2,3,1,0:T(8,128)(2,1)S(1)}, u32[]{:S(2)}, u32[]{:S(2)}) %all-to-all-start) | async-done | bytes 524320 | tf_op jit(solution)/shard_map/all_to_all | solution.py:61
  37.6 0.1 copy.142
  37.8 0.5 copy.76
  38.4 39.3 %conditional.1 = (bf16[16,64,2,128]{3,2,1,0:T(2,128)(2,1)}, bf16[16,64,2,128]{3,2,1,0:T(2,128)(2,1)}) conditional(s32[]{:T(128)} %clamp.3, bf16[16,64,2,128]{3,2,1,0:T(2,128)(2,1)S(1)} %copy.76, bf16[16,64,2,128]{3,2,1,0:T(2,128)(2,1)S(1)} %copy.76, bf16[16,64,2,128]{3,2,1,0:T(2,128)(2,1)S(1)} %copy.76, ...), branch_computations={%region_1.2_spmd, %region_2.3_spmd, %region_3.4_spmd, %region_4.5_... | conditional | bytes 4194400 | solution.py:94
  38.5 8.3 %collective-permute-start.21 = (bf16[16,64,2,128]{3,2,1,0:T(2,128)(2,1)S(1)}, bf16[16,64,2,128]{3,2,1,0:T(2,128)(2,1)}, u32[]{:S(2)}, u32[]{:S(2)}) collective-permute-start(bf16[16,64,2,128]{3,2,1,0:T(2,128)(2,1)S(1)} %param.10), channel_id=1, source_target_pairs={{0,88},{8,80},{16,72},{24,64},{32,120},{40,112},{48,104},{56,96},{... | collective-permute-start | bytes 1572872 | tf_op jit(solution)/shard_map/cond/branch_10_fun/ppermute | solution.py:88
  46.8 2.5 %collective-permute-start.20 = (bf16[16,64,2,128]{3,2,1,0:T(2,128)(2,1)S(1)}, bf16[16,64,2,128]{3,2,1,0:T(2,128)(2,1)}, u32[]{:S(2)}, u32[]{:S(2)}) collective-permute-start(bf16[16,64,2,128]{3,2,1,0:T(2,128)(2,1)S(1)} %param.10), channel_id=1, source_target_pairs={{0,504},{8,496},{16,488},{24,480},{32,472},{40,464},{48,456},{56,4... | collective-permute-start | bytes 1572872 | tf_op jit(solution)/shard_map/cond/branch_10_fun/ppermute | solution.py:87
  49.3 25.4 %collective-permute-done.21 = bf16[16,64,2,128]{3,2,1,0:T(2,128)(2,1)} collective-permute-done((bf16[16,64,2,128]{3,2,1,0:T(2,128)(2,1)S(1)}, bf16[16,64,2,128]{3,2,1,0:T(2,128)(2,1)}, u32[]{:S(2)}, u32[]{:S(2)}) %collective-permute-start.21) | collective-permute-done | bytes 524320 | tf_op jit(solution)/shard_map/cond/branch_10_fun/ppermute | solution.py:88
  74.7 3.1 %collective-permute-done.20 = bf16[16,64,2,128]{3,2,1,0:T(2,128)(2,1)} collective-permute-done((bf16[16,64,2,128]{3,2,1,0:T(2,128)(2,1)S(1)}, bf16[16,64,2,128]{3,2,1,0:T(2,128)(2,1)}, u32[]{:S(2)}, u32[]{:S(2)}) %collective-permute-start.20) | collective-permute-done | bytes 524320 | tf_op jit(solution)/shard_map/cond/branch_10_fun/ppermute | solution.py:87
  77.8 1.3 %broadcast_select_fusion = (bf16[16,16,8,128]{3,2,1,0:T(8,128)(2,1)S(1)}, bf16[16,16,8,128]{3,2,1,0:T(8,128)(2,1)S(1)}) fusion(bf16[16,16,8,128]{3,2,1,0:T(8,128)(2,1)} %bitcast.47, bf16[16,16,8,128]{3,2,1,0:T(8,128)(2,1)} %bitcast.48, pred[]{:T(512)S(6)} %eq.11, pred[]{:T(512)S(6)} %eq.10), kind=kLoop, calls=%fused_computation.10 | loop fusion | flops 524288 | bytes 2097154 | tf_op jit(solution)/shard_map/jit(_where)/select_n | solution.py:100
  79.0 1.1 %slice_convert_fusion.1 = (f32[16,64,1,128]{3,2,1,0:T(1,128)S(1)}, f32[16,64,1,128]{3,2,1,0:T(1,128)S(1)}) fusion(bf16[16,64,2,128]{3,2,1,0:T(2,128)(2,1)S(1)} %bitcast.55), kind=kLoop, calls=%fused_computation.17 | loop fusion | flops 262144 | bytes 1572864 | tf_op jit(solution)/shard_map/convert_element_type | solution.py:71
  80.1 1.1 %slice_convert_fusion.3 = (f32[16,64,1,128]{3,2,1,0:T(1,128)S(1)}, f32[16,64,1,128]{3,2,1,0:T(1,128)S(1)}) fusion(bf16[16,64,2,128]{3,2,1,0:T(2,128)(2,1)S(1)} %bitcast.54), kind=kLoop, calls=%fused_computation.19 | loop fusion | flops 262144 | bytes 1572864 | tf_op jit(solution)/shard_map/convert_element_type | solution.py:71
  81.2 0.1 broadcast_select_fusion.2
  81.3 6.3 %add_reduce_fusion.2 = (f32[16,16,128]{2,1,0:T(8,128)S(1)}, f32[16,16,128]{2,1,0:T(8,128)S(1)}, f32[16,16,128]{2,1,0:T(8,128)S(1)}) fusion(f32[16,64,128]{2,1,0:T(8,128)S(1)} %get-tuple-element.83, f32[16,64,128]{2,1,0:T(8,128)S(1)} %get-tuple-element.81, f32[16,64,128]{2,1,0:T(8,128)S(1)} %get-tuple-element.82, f32[16,64,128]{2,1,0:T(8,128)S(1)} %get-tuple-element.80, ...), kind=kLoop, calls=%fused_computation.2 | loop fusion | flops 25067520 | bytes 4587520 | tf_op jit(solution)/shard_map/reduce_sum | solution.py:73
  87.7 0.8 copy.138
  (11 shorter events, 0.3 us)
Async XLA Ops:
  1.0 7.3 %collective-permute-start.124 = (bf16[16,3,1024]{2,1,0:T(4,128)(2,1)S(1)}, bf16[16,3,1024]{2,1,0:T(4,128)(2,1)S(1)}, u32[]{:S(2)}, u32[]{:S(2)}) collective-permute-start(bf16[16,3,1024]{2,1,0:T(4,128)(2,1)S(1)} %slice.58), channel_id=1, source_target_pairs={{0,1},{1,2},{2,3},{3,4},{4,5},{5,6},{6,7},{8,9},{9,10},{10,11},{11... | collective-permute-start | bytes 294920 | tf_op jit(solution)/shard_map/ppermute | solution.py:15
  3.6 0.7 copy-start.1
  3.6 4.7 %copy-start = (bf16[16,8,1024]{2,1,0:T(8,128)(2,1)S(1)}, bf16[16,8,1024]{2,1,0:T(8,128)(2,1)}, u32[]{:S(2)}) copy-start(bf16[16,8,1024]{2,1,0:T(8,128)(2,1)} %param.65) | copy-start | bytes 786436
  11.1 10.7 %copy-start.2 = (s32[2]{0:T(128)S(1)}, s32[2]{0:T(128)}, u32[]{:S(2)}) copy-start(s32[2]{0:T(128)} %param.67) | copy-start | bytes 28
  11.9 25.7 %all-to-all-start = ((bf16[8,16,8,2,128]{4,2,3,1,0:T(8,128)(2,1)}), bf16[8,16,8,2,128]{4,2,3,1,0:T(8,128)(2,1)S(1)}, u32[]{:S(2)}, u32[]{:S(2)}) async-start(bf16[8,16,8,2,128]{4,2,3,1,0:T(8,128)(2,1)} %pad_maximum_fusion), calls=%async_computation | async-start | bytes 1048576 | tf_op jit(solution)/shard_map/all_to_all | solution.py:61
  38.5 36.2 %collective-permute-start.21 = (bf16[16,64,2,128]{3,2,1,0:T(2,128)(2,1)S(1)}, bf16[16,64,2,128]{3,2,1,0:T(2,128)(2,1)}, u32[]{:S(2)}, u32[]{:S(2)}) collective-permute-start(bf16[16,64,2,128]{3,2,1,0:T(2,128)(2,1)S(1)} %param.10), channel_id=1, source_target_pairs={{0,88},{8,80},{16,72},{24,64},{32,120},{40,112},{48,104},{56,96},{... | collective-permute-start | bytes 1572872 | tf_op jit(solution)/shard_map/cond/branch_10_fun/ppermute | solution.py:88
  46.8 31.0 %collective-permute-start.20 = (bf16[16,64,2,128]{3,2,1,0:T(2,128)(2,1)S(1)}, bf16[16,64,2,128]{3,2,1,0:T(2,128)(2,1)}, u32[]{:S(2)}, u32[]{:S(2)}) collective-permute-start(bf16[16,64,2,128]{3,2,1,0:T(2,128)(2,1)S(1)} %param.10), channel_id=1, source_target_pairs={{0,504},{8,496},{16,488},{24,480},{32,472},{40,464},{48,456},{56,4... | collective-permute-start | bytes 1572872 | tf_op jit(solution)/shard_map/cond/branch_10_fun/ppermute | solution.py:87

commit v2 on v1

--- a/solution.py
+++ b/solution.py
@@ -59,28 +59,25 @@
     grouped = jnp.transpose(grouped, (3, 0, 1, 2, 4))
     send = jnp.concatenate([grouped] * (tm_size // chunks), axis=0)
     got = lax.all_to_all(send, "tm", 0, 0, tiled=True)
-    got = jnp.transpose(got, (1, 0, 2, 3, 4))
-    return got.reshape(in_dev, tm_size * spec_dev, both_parts, width)
-
-
-def column_terms(left, right, imag_half):
-    left_re = left[:, :, 0, :].astype(jnp.float32)
-    left_im = left[:, :, 1, :].astype(jnp.float32)
-    first = jnp.where(imag_half, left_im, left_re)
-    second = jnp.where(imag_half, -left_re, left_im)
-    right_re = right[None, :, :, 0, :].astype(jnp.float32)
-    right_im = right[None, :, :, 1, :].astype(jnp.float32)
-    return jnp.sum(first[:, None] * right_re + second[:, None] * right_im, axis=2)
+    got = jnp.transpose(got, (4, 1, 3, 0, 2))
+    return got.reshape(width, in_dev, both_parts * tm_size * spec_dev)
 
 
 def on_device(samples, filter_taps, partner_mask):
     spectra = channelize(samples, filter_taps)
     tm_size = lax.axis_size("tm")
     own_block = by_channel_chunk(spectra, tm_size)
-    norm_scale = 1.0 / own_block.shape[1]
+    half = own_block.shape[2] // 2
+    norm_scale = 1.0 / half
     inp_size = lax.axis_size("inp")
     all_bits = inp_size - 1
     imag_half = lax.axis_index("tm") >= tm_size // 2
+    swapped = jnp.concatenate([own_block[..., half:], -own_block[..., :half]], axis=-1)
+    left = jnp.where(imag_half, swapped, own_block)
+
+    def column_terms(right):
+        term = jnp.einsum("cix,cjx->ijc", left, right, preferred_element_type=jnp.float32)
+        return term * norm_scale
 
     def exchange(m):
         def both(x):
@@ -94,12 +91,13 @@
     full_partner, other_partner = lax.switch(
         jnp.clip(other_mask - 1, 0, all_bits - 2), branches, own_block
     )
-    pair_terms = [column_terms(own_block, own_block, imag_half)]
+    full_term = column_terms(full_partner)
+    other_term = column_terms(other_partner)
+    pair_terms = [column_terms(own_block)]
     for round_index in range(ROUNDS):
         is_full = partner_mask[round_index] == all_bits
-        partner = jnp.where(is_full, full_partner, other_partner)
-        pair_terms.append(column_terms(own_block, partner, imag_half))
-    return jnp.stack(pair_terms, axis=1) * norm_scale
+        pair_terms.append(jnp.where(is_full, full_term, other_term))
+    return jnp.stack(pair_terms, axis=1)
 
 
 def solution(mesh):

time: 88.8 us -> 87.1 us (0.981)
  the two profiles are of different devices: /device:TPU:80 before, /device:TPU:88 now
where the time goes in v2:
time: 87.1 us; the launch traced here: 86.7 us
  waiting for transfers between devices  42.8 us (49%)
  starting transfers between devices  27.7 us (32%)
  matrix products  6.04 us (7%)
  local copies, waits for them, and re-layouts  4.11 us (5%)
  other arithmetic  3.08 us (4%)
  between operations  2.83 us (3%)
    ppermute x1, waiting for transfers between devices, both(): full = lax.ppermute(x, 'inp', [(i, i ^ all_bits) for i in range(inp_size)])  19.4 us
    ppermute x1, starting transfers between devices, both(): full = lax.ppermute(x, 'inp', [(i, i ^ all_bits) for i in range(inp_size)])  16.9 us
    all_to_all x1, waiting for transfers between devices, by_channel_chunk(): got = lax.all_to_all(send, 'tm', 0, 0, tiled=True)  9.78 us
    ppermute x1, waiting for transfers between devices, both(): other = lax.ppermute(x, 'inp', [(i, i ^ m) for i in range(inp_size)])  8.35 us
    all_to_all x1, starting transfers between devices, by_channel_chunk(): got = lax.all_to_all(send, 'tm', 0, 0, tiled=True)  6.52 us
    ppermute x1, waiting for transfers between devices, shifted(): return lax.ppermute(block, axis, route)  5.28 us
    dot_general x3, matrix products, column_terms(): jnp.einsum('cix,cjx->ijc', left, right, preferred_element_type=jnp.float32)  3.3 us
    dot_general x1, matrix products, channelize(): jnp.dot(filtered.reshape(in_dev * spec_dev, n_fft), dft_table, precision=...  2.74 us
  transfers between devices with their start and end apart: 4, of which 4 were waited for; matrix products, arithmetic and copies ran while one was open for 2% of the time, Pallas kernels for 0%

profile of v2, /device:TPU:88, one launch (start us, length us, event | category | flops | bytes accessed | tf_op | source)
XLA Modules:
  0.0 86.7 jit_solution(761888209613346905)
XLA Ops:
  0.0 1.0 %slice.40 = bf16[16,3,1024]{2,1,0:T(4,128)(2,1)S(1)} slice(bf16[16,8,1024]{2,1,0:T(8,128)(2,1)} %param.65), slice={[0:16], [5:8], [0:1024]} | slice | bytes 196608 | tf_op jit(solution)/shard_map/slice | solution.py:37
  1.0 1.9 %collective-permute-start.124 = (bf16[16,3,1024]{2,1,0:T(4,128)(2,1)S(1)}, bf16[16,3,1024]{2,1,0:T(4,128)(2,1)S(1)}, u32[]{:S(2)}, u32[]{:S(2)}) collective-permute-start(bf16[16,3,1024]{2,1,0:T(4,128)(2,1)S(1)} %slice.40), channel_id=1, source_target_pairs={{0,1},{1,2},{2,3},{3,4},{4,5},{5,6},{6,7},{8,9},{9,10},{10,11},{11... | collective-permute-start | bytes 294920 | tf_op jit(solution)/shard_map/ppermute | solution.py:15
  3.2 0.3 fusion.44
  3.6 0.6 multiply_subtract_fusion
  4.3 5.3 %collective-permute-done.124 = bf16[16,3,1024]{2,1,0:T(4,128)(2,1)S(1)} collective-permute-done((bf16[16,3,1024]{2,1,0:T(4,128)(2,1)S(1)}, bf16[16,3,1024]{2,1,0:T(4,128)(2,1)S(1)}, u32[]{:S(2)}, u32[]{:S(2)}) %collective-permute-start.124) | collective-permute-done | bytes 98336 | tf_op jit(solution)/shard_map/ppermute | solution.py:15
  9.6 2.7 %fusion.5 = bf16[128,1024]{1,0:T(8,128)(2,1)S(1)} fusion(f32[1024,512]{1,0:T(8,128)S(1)} %bitcast.40, f32[1024,512]{1,0:T(8,128)S(1)} %bitcast.39, bf16[16,8,1024]{2,1,0:T(8,128)(2,1)S(1)} %copy-done, bf16[16,3,1024]{2,1,0:T(4,128)(2,1)S(1)} %collective-permute-done.124, f32[1024]{0:T(1024)S(1)} %bitcast.45, f32[1024]{0:T(1024)S(1)} %bitcast.46, ...), kind=kOutput, calls=%fused_computation.10 | convolution fusion | flops 1614413824 | bytes 4833280 | tf_op jit(solution)/shard_map/dot_general | solution.py:45
  12.4 0.8 pad_maximum_fusion
  13.3 6.5 %all-to-all-start = ((bf16[8,16,8,2,128]{4,2,3,1,0:T(8,128)(2,1)}), bf16[8,16,8,2,128]{4,2,3,1,0:T(8,128)(2,1)S(1)}, u32[]{:S(2)}, u32[]{:S(2)}) async-start(bf16[8,16,8,2,128]{4,2,3,1,0:T(8,128)(2,1)} %pad_maximum_fusion), calls=%async_computation | async-start | bytes 1048576 | tf_op jit(solution)/shard_map/all_to_all | solution.py:61
  19.8 0.6 fusion.49
  23.1 9.8 %all-to-all-done = bf16[8,16,8,2,128]{4,2,3,1,0:T(8,128)(2,1)S(1)} async-done(((bf16[8,16,8,2,128]{4,2,3,1,0:T(8,128)(2,1)}), bf16[8,16,8,2,128]{4,2,3,1,0:T(8,128)(2,1)S(1)}, u32[]{:S(2)}, u32[]{:S(2)}) %all-to-all-start) | async-done | bytes 524320 | tf_op jit(solution)/shard_map/all_to_all | solution.py:61
  33.0 0.4 copy.75
  33.7 0.4 copy.76
  34.1 0.4 fusion.4
  34.5 0.4 copy.141
  35.0 47.1 %conditional.1 = (bf16[128,16,128]{2,1,0:T(8,128)(2,1)}, bf16[128,16,128]{2,1,0:T(8,128)(2,1)}) conditional(s32[]{:T(128)} %clamp.3, bf16[128,16,128]{2,1,0:T(8,128)(2,1)S(1)} %copy.75, bf16[128,16,128]{2,1,0:T(8,128)(2,1)S(1)} %copy.75, bf16[128,16,128]{2,1,0:T(8,128)(2,1)S(1)} %copy.75, ...), branch_computations={%region_0.1_spmd, %region_1.2_spmd, %region_2.3_spmd, %region_3.4_... | conditional | bytes 4194400 | solution.py:91
  35.0 16.9 %collective-permute-start.28 = (bf16[128,16,128]{2,1,0:T(8,128)(2,1)S(1)}, bf16[128,16,128]{2,1,0:T(8,128)(2,1)}, u32[]{:S(2)}, u32[]{:S(2)}) collective-permute-start(bf16[128,16,128]{2,1,0:T(8,128)(2,1)S(1)} %param.14), channel_id=1, source_target_pairs={{0,504},{8,496},{16,488},{24,480},{32,472},{40,464},{48,456},{56,4... | collective-permute-start | bytes 1572872 | tf_op jit(solution)/shard_map/cond/branch_14_fun/ppermute | solution.py:84
  51.9 2.4 %collective-permute-start.29 = (bf16[128,16,128]{2,1,0:T(8,128)(2,1)S(1)}, bf16[128,16,128]{2,1,0:T(8,128)(2,1)}, u32[]{:S(2)}, u32[]{:S(2)}) collective-permute-start(bf16[128,16,128]{2,1,0:T(8,128)(2,1)S(1)} %param.14), channel_id=1, source_target_pairs={{0,120},{8,112},{16,104},{24,96},{32,88},{40,80},{48,72},{56,64},{... | collective-permute-start | bytes 1572872 | tf_op jit(solution)/shard_map/cond/branch_14_fun/ppermute | solution.py:85
  54.3 19.4 %collective-permute-done.28 = bf16[128,16,128]{2,1,0:T(8,128)(2,1)} collective-permute-done((bf16[128,16,128]{2,1,0:T(8,128)(2,1)S(1)}, bf16[128,16,128]{2,1,0:T(8,128)(2,1)}, u32[]{:S(2)}, u32[]{:S(2)}) %collective-permute-start.28) | collective-permute-done | bytes 524320 | tf_op jit(solution)/shard_map/cond/branch_14_fun/ppermute | solution.py:84
  73.7 8.4 %collective-permute-done.29 = bf16[128,16,128]{2,1,0:T(8,128)(2,1)} collective-permute-done((bf16[128,16,128]{2,1,0:T(8,128)(2,1)S(1)}, bf16[128,16,128]{2,1,0:T(8,128)(2,1)}, u32[]{:S(2)}, u32[]{:S(2)}) %collective-permute-start.29) | collective-permute-done | bytes 524320 | tf_op jit(solution)/shard_map/cond/branch_14_fun/ppermute | solution.py:85
  82.1 1.4 %convolution_multiply_fusion = f32[128,16,16]{2,1,0:T(8,128)S(1)} fusion(bf16[128,16,128]{2,1,0:T(8,128)(2,1)} %get-tuple-element.70, bf16[128,16,128]{2,1,0:T(8,128)(2,1)S(1)} %copy.76), kind=kOutput, calls=%fused_computation.6 | convolution fusion | flops 8421376 | bytes 1179648 | tf_op jit(solution)/shard_map/cix,cjx->ijc/dot_general | solution.py:79
  83.5 1.5 %select_bitcast_fusion.1 = (f32[16,1,16,128]{0,2,3,1:T(8,128)S(1)}, f32[16,1,16,128]{0,2,3,1:T(8,128)S(1)}) fusion(f32[128,16,16]{2,1,0:T(8,128)S(1)} %convolution_multiply_fusion, pred[]{:T(512)S(6)} %eq.10, pred[]{:T(512)S(6)} %eq.11, bf16[128,16,128]{2,1,0:T(8,128)(2,1)} %get-tuple-element.69, bf16[128,16,128]{2,1,0:T(8,128)(2,1)S(1)} %copy.76), kind=kOutput, calls=%fused_computation.12 | convolution fusion | flops 8486912 | bytes 1441794 | tf_op jit(solution)/shard_map/cix,cjx->ijc/dot_general | solution.py:79
  85.0 0.4 copy.142
  85.4 0.4 copy.143
  85.9 0.8 pad_maximum_fusion.1
  (13 shorter events, 0.8 us)
Async XLA Ops:
  1.0 8.6 %collective-permute-start.124 = (bf16[16,3,1024]{2,1,0:T(4,128)(2,1)S(1)}, bf16[16,3,1024]{2,1,0:T(4,128)(2,1)S(1)}, u32[]{:S(2)}, u32[]{:S(2)}) collective-permute-start(bf16[16,3,1024]{2,1,0:T(4,128)(2,1)S(1)} %slice.40), channel_id=1, source_target_pairs={{0,1},{1,2},{2,3},{3,4},{4,5},{5,6},{6,7},{8,9},{9,10},{10,11},{11... | collective-permute-start | bytes 294920 | tf_op jit(solution)/shard_map/ppermute | solution.py:15
  3.6 0.7 copy-start.1
  3.6 6.0 %copy-start = (bf16[16,8,1024]{2,1,0:T(8,128)(2,1)S(1)}, bf16[16,8,1024]{2,1,0:T(8,128)(2,1)}, u32[]{:S(2)}) copy-start(bf16[16,8,1024]{2,1,0:T(8,128)(2,1)} %param.65) | copy-start | bytes 786436
  12.3 7.4 %copy-start.2 = (s32[2]{0:T(128)S(1)}, s32[2]{0:T(128)}, u32[]{:S(2)}) copy-start(s32[2]{0:T(128)} %param.67) | copy-start | bytes 28
  13.3 19.6 %all-to-all-start = ((bf16[8,16,8,2,128]{4,2,3,1,0:T(8,128)(2,1)}), bf16[8,16,8,2,128]{4,2,3,1,0:T(8,128)(2,1)S(1)}, u32[]{:S(2)}, u32[]{:S(2)}) async-start(bf16[8,16,8,2,128]{4,2,3,1,0:T(8,128)(2,1)} %pad_maximum_fusion), calls=%async_computation | async-start | bytes 1048576 | tf_op jit(solution)/shard_map/all_to_all | solution.py:61
  35.0 38.7 %collective-permute-start.28 = (bf16[128,16,128]{2,1,0:T(8,128)(2,1)S(1)}, bf16[128,16,128]{2,1,0:T(8,128)(2,1)}, u32[]{:S(2)}, u32[]{:S(2)}) collective-permute-start(bf16[128,16,128]{2,1,0:T(8,128)(2,1)S(1)} %param.14), channel_id=1, source_target_pairs={{0,504},{8,496},{16,488},{24,480},{32,472},{40,464},{48,456},{56,4... | collective-permute-start | bytes 1572872 | tf_op jit(solution)/shard_map/cond/branch_14_fun/ppermute | solution.py:84
  51.9 30.2 %collective-permute-start.29 = (bf16[128,16,128]{2,1,0:T(8,128)(2,1)S(1)}, bf16[128,16,128]{2,1,0:T(8,128)(2,1)}, u32[]{:S(2)}, u32[]{:S(2)}) collective-permute-start(bf16[128,16,128]{2,1,0:T(8,128)(2,1)S(1)} %param.14), channel_id=1, source_target_pairs={{0,120},{8,112},{16,104},{24,96},{32,88},{40,80},{48,72},{56,64},{... | collective-permute-start | bytes 1572872 | tf_op jit(solution)/shard_map/cond/branch_14_fun/ppermute | solution.py:85

commit v3 on v1

--- a/solution.py
+++ b/solution.py
@@ -32,22 +32,39 @@
     return jnp.concatenate([cos_ab, -sin_ab], axis=1)
 
 
-def channelize(samples, filter_taps):
-    in_dev, spec_dev, n_fft = samples.shape
-    history = shifted(samples[:, spec_dev - (TAPS - 1) :, :], "tm", 1)
-    frames = jnp.concatenate([history, samples], axis=1)
-    filtered = jnp.zeros((in_dev, spec_dev, n_fft), jnp.float32)
+def filter_frames(frames, filter_taps, count):
+    filtered = jnp.zeros((frames.shape[0], count, frames.shape[2]), jnp.float32)
     for tap_index in range(TAPS):
         filtered = filtered + filter_taps[tap_index][None, None, :] * frames[
-            :, tap_index : tap_index + spec_dev, :
+            :, tap_index : tap_index + count, :
         ].astype(jnp.float32)
-    dft_table = dft_columns(n_fft)
+    return filtered
+
+
+def spectra_of(filtered, dft_table):
+    in_dev, count, n_fft = filtered.shape
     spectra = jnp.dot(
-        filtered.reshape(in_dev * spec_dev, n_fft),
+        filtered.reshape(in_dev * count, n_fft),
         dft_table,
         precision=lax.Precision.HIGHEST,
         preferred_element_type=jnp.float32,
     )
+    return spectra.reshape(in_dev, count, n_fft)
+
+
+def channelize(samples, filter_taps):
+    in_dev, spec_dev, n_fft = samples.shape
+    lead = TAPS - 1
+    history = shifted(samples[:, spec_dev - lead :, :], "tm", 1)
+    blank = jnp.zeros((in_dev, lead, n_fft), samples.dtype)
+    dft_table = dft_columns(n_fft)
+    local_part = spectra_of(
+        filter_frames(jnp.concatenate([blank, samples], axis=1), filter_taps, spec_dev), dft_table
+    )
+    history_part = spectra_of(
+        filter_frames(jnp.concatenate([history, blank], axis=1), filter_taps, lead), dft_table
+    )
+    spectra = jnp.concatenate([local_part[:, :lead] + history_part, local_part[:, lead:]], axis=1)
     return spectra.astype(jnp.bfloat16).reshape(in_dev, spec_dev, 2, n_fft // 2)
 
 
@@ -94,11 +111,12 @@
     full_partner, other_partner = lax.switch(
         jnp.clip(other_mask - 1, 0, all_bits - 2), branches, own_block
     )
+    full_term = column_terms(own_block, full_partner, imag_half)
+    other_term = column_terms(own_block, other_partner, imag_half)
     pair_terms = [column_terms(own_block, own_block, imag_half)]
     for round_index in range(ROUNDS):
         is_full = partner_mask[round_index] == all_bits
-        partner = jnp.where(is_full, full_partner, other_partner)
-        pair_terms.append(column_terms(own_block, partner, imag_half))
+        pair_terms.append(jnp.where(is_full, full_term, other_term))
     return jnp.stack(pair_terms, axis=1) * norm_scale
 
 

time: 88.8 us -> 112 us (1.26)
  the two profiles are of different devices: /device:TPU:80 before, /device:TPU:1 now
where the time goes in v3:
time: 112 us; the launch traced here: 111 us
  waiting for transfers between devices  56.1 us (50%)
  starting transfers between devices  26.7 us (24%)
  other arithmetic  12.6 us (11%)
  matrix products  6.82 us (6%)
  local copies, waits for them, and re-layouts  6.16 us (6%)
  between operations  2.93 us (3%)
    ppermute x1, waiting for transfers between devices, both(): other = lax.ppermute(x, 'inp', [(i, i ^ m) for i in range(inp_size)])  22.5 us
    ppermute x1, waiting for transfers between devices, both(): full = lax.ppermute(x, 'inp', [(i, i ^ all_bits) for i in range(inp_size)])  21.2 us
    all_to_all x1, waiting for transfers between devices, by_channel_chunk(): got = lax.all_to_all(send, 'tm', 0, 0, tiled=True)  12.4 us
    ppermute x1, starting transfers between devices, both(): full = lax.ppermute(x, 'inp', [(i, i ^ all_bits) for i in range(inp_size)])  12.3 us
    dot_general x2, matrix products, spectra_of(): jnp.dot(filtered.reshape(in_dev * count, n_fft), dft_table, precision=lax...  6.82 us
    all_to_all x1, starting transfers between devices, by_channel_chunk(): got = lax.all_to_all(send, 'tm', 0, 0, tiled=True)  6.36 us
    reduce_sum x1, other arithmetic, column_terms(): jnp.sum(first[:, None] * right_re + second[:, None] * right_im, axis=2)  6.35 us
    ppermute x1, starting transfers between devices, shifted(): return lax.ppermute(block, axis, route)  5.61 us
  transfers between devices with their start and end apart: 4, of which 3 were waited for; matrix products, arithmetic and copies ran while one was open for 5% of the time, Pallas kernels for 0%

profile of v3, /device:TPU:1, one launch (start us, length us, event | category | flops | bytes accessed | tf_op | source)
XLA Modules:
  0.0 111.4 jit_solution(7257125371594624557)
XLA Ops:
  0.0 1.0 slice.82
  1.1 5.6 %collective-permute-start.124 = (bf16[16,3,1024]{2,0,1:T(8,128)(2,1)S(1)}, bf16[16,3,1024]{2,0,1:T(8,128)(2,1)S(1)}, u32[]{:S(2)}, u32[]{:S(2)}) collective-permute-start(bf16[16,3,1024]{2,0,1:T(8,128)(2,1)S(1)} %copy.296), channel_id=1, source_target_pairs={{0,1},{1,2},{2,3},{3,4},{4,5},{5,6},{6,7},{8,9},{9,10},{10,11},{11... | collective-permute-start | bytes 294920 | tf_op jit(solution)/shard_map/ppermute | solution.py:15
  6.7 0.3 fusion.46
  7.0 0.3 fusion.49
  7.3 0.9 fusion.54
  8.2 0.5 multiply_subtract_fusion
  8.7 0.4 copy-done.1
  9.2 2.6 %fusion.1 = f32[16,8,1024]{2,1,0:T(8,128)S(1)} fusion(f32[1024,512]{1,0:T(8,128)S(1)} %bitcast.57, f32[1024,512]{1,0:T(8,128)S(1)} %bitcast.55, bf16[16,8,1024]{2,1,0:T(8,128)(2,1)S(1)} %copy-done.1, f32[1024]{0:T(1024)S(1)} %bitcast.75, f32[1024]{0:T(1024)S(1)} %bitcast.73, f32[1024]{0:T(1024)S(1)} %bitcast.71, f32[1024]{0:T(1024)S(1)} %bitcast.69), kind=kOutput, calls=%fused_computation.5 | convolution fusion | flops 1613103104 | bytes 4997120 | tf_op jit(solution)/shard_map/dot_general | solution.py:46
  12.0 4.2 %fusion.3 = bf16[16,3,1024]{2,0,1:T(8,128)(2,1)S(1)} fusion(f32[1024,512]{1,0:T(8,128)} %bitcast.58, f32[1024,512]{1,0:T(8,128)S(1)} %bitcast.56, f32[16,3,1024]{2,1,0:T(4,128)S(1)} %slice.94, bf16[16,3,1024]{2,0,1:T(8,128)(2,1)S(1)} %collective-permute-done.124, f32[1024]{0:T(1024)S(1)} %broadcast_multiply_fusion, f32[1024]{0:T(1024)S(1)} %bitcast.74, ...), kind=kOutput, calls=%fused_computation.9 | convolution fusion | flops 605569024 | bytes 4603904 | tf_op jit(solution)/shard_map/dot_general | solution.py:46
  16.5 0.2 pad_maximum_fusion
  16.7 1.2 %copy.227 = bf16[8,16,8,2,128]{4,3,1,2,0:T(2,128)(2,1)} copy(bf16[8,16,8,2,128]{4,0,3,1,2:T(8,128)(2,1)S(1)} %pad_maximum_fusion) | data formatting | bytes 1048576 | tf_op jit(solution)/shard_map/concatenate | solution.py:77
  17.9 6.4 %all-to-all-start = ((bf16[8,16,8,2,128]{4,3,1,2,0:T(2,128)(2,1)}), bf16[8,16,8,2,128]{4,3,1,2,0:T(2,128)(2,1)S(1)}, u32[]{:S(2)}, u32[]{:S(2)}) async-start(bf16[8,16,8,2,128]{4,3,1,2,0:T(2,128)(2,1)} %copy.227), calls=%async_computation | async-start | bytes 1048576 | tf_op jit(solution)/shard_map/all_to_all | solution.py:78
  24.3 0.6 fusion.55
  27.6 12.4 %all-to-all-done = bf16[8,16,8,2,128]{4,3,1,2,0:T(2,128)(2,1)S(1)} async-done(((bf16[8,16,8,2,128]{4,3,1,2,0:T(2,128)(2,1)}), bf16[8,16,8,2,128]{4,3,1,2,0:T(2,128)(2,1)S(1)}, u32[]{:S(2)}, u32[]{:S(2)}) %all-to-all-start) | async-done | bytes 524320 | tf_op jit(solution)/shard_map/all_to_all | solution.py:78
  40.1 0.5 copy.230
  40.7 58.5 %conditional.1 = (bf16[16,64,2,128]{3,2,1,0:T(2,128)(2,1)}, bf16[16,64,2,128]{3,2,1,0:T(2,128)(2,1)}) conditional(s32[]{:T(128)} %clamp.3, bf16[16,64,2,128]{3,2,1,0:T(2,128)(2,1)S(1)} %copy.230, bf16[16,64,2,128]{3,2,1,0:T(2,128)(2,1)S(1)} %copy.230, bf16[16,64,2,128]{3,2,1,0:T(2,128)(2,1)S(1)} %copy.230, ...), branch_computations={%region_1.2_spmd, %region_2.3_spmd, %region_3.4_spmd, %region_4.5_... | conditional | bytes 4194400 | solution.py:111
  40.8 12.3 %collective-permute-start.44 = (bf16[16,64,2,128]{3,2,1,0:T(2,128)(2,1)S(1)}, bf16[16,64,2,128]{3,2,1,0:T(2,128)(2,1)}, u32[]{:S(2)}, u32[]{:S(2)}) collective-permute-start(bf16[16,64,2,128]{3,2,1,0:T(2,128)(2,1)S(1)} %param.22), channel_id=1, source_target_pairs={{0,504},{8,496},{16,488},{24,480},{32,472},{40,464},{48,456},{56,4... | collective-permute-start | bytes 1572872 | tf_op jit(solution)/shard_map/cond/branch_22_fun/ppermute | solution.py:104
  53.1 2.5 %collective-permute-start.45 = (bf16[16,64,2,128]{3,2,1,0:T(2,128)(2,1)S(1)}, bf16[16,64,2,128]{3,2,1,0:T(2,128)(2,1)}, u32[]{:S(2)}, u32[]{:S(2)}) collective-permute-start(bf16[16,64,2,128]{3,2,1,0:T(2,128)(2,1)S(1)} %param.22), channel_id=1, source_target_pairs={{0,184},{8,176},{16,168},{24,160},{32,152},{40,144},{48,136},{56,1... | collective-permute-start | bytes 1572872 | tf_op jit(solution)/shard_map/cond/branch_22_fun/ppermute | solution.py:105
  55.6 21.2 %collective-permute-done.44 = bf16[16,64,2,128]{3,2,1,0:T(2,128)(2,1)} collective-permute-done((bf16[16,64,2,128]{3,2,1,0:T(2,128)(2,1)S(1)}, bf16[16,64,2,128]{3,2,1,0:T(2,128)(2,1)}, u32[]{:S(2)}, u32[]{:S(2)}) %collective-permute-start.44) | collective-permute-done | bytes 524320 | tf_op jit(solution)/shard_map/cond/branch_22_fun/ppermute | solution.py:104
  76.7 22.5 %collective-permute-done.45 = bf16[16,64,2,128]{3,2,1,0:T(2,128)(2,1)} collective-permute-done((bf16[16,64,2,128]{3,2,1,0:T(2,128)(2,1)S(1)}, bf16[16,64,2,128]{3,2,1,0:T(2,128)(2,1)}, u32[]{:S(2)}, u32[]{:S(2)}) %collective-permute-start.45) | collective-permute-done | bytes 524320 | tf_op jit(solution)/shard_map/cond/branch_22_fun/ppermute | solution.py:105
  99.3 2.2 %slice_convert_fusion.4 = (f32[16,64,1,128]{3,2,1,0:T(1,128)S(1)}, f32[16,64,1,128]{3,2,1,0:T(1,128)S(1)}) fusion(bf16[16,64,2,128]{3,2,1,0:T(2,128)(2,1)} %get-tuple-element.69), kind=kLoop, calls=%fused_computation.20 | loop fusion | flops 262144 | bytes 1572864 | tf_op jit(solution)/shard_map/convert_element_type | solution.py:88
  101.5 2.2 %slice_convert_fusion.2 = (f32[16,64,1,128]{3,2,1,0:T(1,128)S(1)}, f32[16,64,1,128]{3,2,1,0:T(1,128)S(1)}) fusion(bf16[16,64,2,128]{3,2,1,0:T(2,128)(2,1)} %get-tuple-element.70), kind=kLoop, calls=%fused_computation.18 | loop fusion | flops 262144 | bytes 1572864 | tf_op jit(solution)/shard_map/convert_element_type | solution.py:88
  104.2 6.3 %add_reduce_fusion.2 = (f32[16,16,128]{2,1,0:T(8,128)S(1)}, f32[16,16,128]{2,1,0:T(8,128)S(1)}, f32[16,16,128]{2,1,0:T(8,128)S(1)}) fusion(f32[16,64,128]{2,1,0:T(8,128)S(1)} %fusion.16, f32[16,64,128]{2,1,0:T(8,128)S(1)} %get-tuple-element.75, f32[16,64,128]{2,1,0:T(8,128)S(1)} %fusion.15, f32[16,64,128]{2,1,0:T(8,128)S(1)} %get-tuple-element.74, ...), kind=kLoop, calls=%fused_computation.2 | loop fusion | flops 25067520 | bytes 4587520 | tf_op jit(solution)/shard_map/reduce_sum | solution.py:90
  110.6 0.8 copy.292
  (21 shorter events, 1.1 us)
Async XLA Ops:
  1.1 10.9 %collective-permute-start.124 = (bf16[16,3,1024]{2,0,1:T(8,128)(2,1)S(1)}, bf16[16,3,1024]{2,0,1:T(8,128)(2,1)S(1)}, u32[]{:S(2)}, u32[]{:S(2)}) collective-permute-start(bf16[16,3,1024]{2,0,1:T(8,128)(2,1)S(1)} %copy.296), channel_id=1, source_target_pairs={{0,1},{1,2},{2,3},{3,4},{4,5},{5,6},{6,7},{8,9},{9,10},{10,11},{11... | collective-permute-start | bytes 294920 | tf_op jit(solution)/shard_map/ppermute | solution.py:15
  8.2 1.0 copy-start.1
  8.7 3.0 %copy-start = (f32[32,32,512]{2,1,0:T(8,128)}, f32[32,32,512]{2,1,0:T(8,128)S(1)}, u32[]{:S(2)}) copy-start(f32[32,32,512]{2,1,0:T(8,128)S(1)} %get-tuple-element.83) | copy-start | bytes 6291460
  16.3 8.0 %copy-start.2 = (s32[2]{0:T(128)S(1)}, s32[2]{0:T(128)}, u32[]{:S(2)}) copy-start(s32[2]{0:T(128)} %param.67) | copy-start | bytes 28
  17.9 22.0 %all-to-all-start = ((bf16[8,16,8,2,128]{4,3,1,2,0:T(2,128)(2,1)}), bf16[8,16,8,2,128]{4,3,1,2,0:T(2,128)(2,1)S(1)}, u32[]{:S(2)}, u32[]{:S(2)}) async-start(bf16[8,16,8,2,128]{4,3,1,2,0:T(2,128)(2,1)} %copy.227), calls=%async_computation | async-start | bytes 1048576 | tf_op jit(solution)/shard_map/all_to_all | solution.py:78
  40.8 35.9 %collective-permute-start.44 = (bf16[16,64,2,128]{3,2,1,0:T(2,128)(2,1)S(1)}, bf16[16,64,2,128]{3,2,1,0:T(2,128)(2,1)}, u32[]{:S(2)}, u32[]{:S(2)}) collective-permute-start(bf16[16,64,2,128]{3,2,1,0:T(2,128)(2,1)S(1)} %param.22), channel_id=1, source_target_pairs={{0,504},{8,496},{16,488},{24,480},{32,472},{40,464},{48,456},{56,4... | collective-permute-start | bytes 1572872 | tf_op jit(solution)/shard_map/cond/branch_22_fun/ppermute | solution.py:104
  53.1 46.2 %collective-permute-start.45 = (bf16[16,64,2,128]{3,2,1,0:T(2,128)(2,1)S(1)}, bf16[16,64,2,128]{3,2,1,0:T(2,128)(2,1)}, u32[]{:S(2)}, u32[]{:S(2)}) collective-permute-start(bf16[16,64,2,128]{3,2,1,0:T(2,128)(2,1)S(1)} %param.22), channel_id=1, source_target_pairs={{0,184},{8,176},{16,168},{24,160},{32,152},{40,144},{48,136},{56,1... | collective-permute-start | bytes 1572872 | tf_op jit(solution)/shard_map/cond/branch_22_fun/ppermute | solution.py:105

commit v4 on v2

--- a/solution.py
+++ b/solution.py
@@ -66,6 +66,7 @@
 def on_device(samples, filter_taps, partner_mask):
     spectra = channelize(samples, filter_taps)
     tm_size = lax.axis_size("tm")
+    in_dev = spectra.shape[0]
     own_block = by_channel_chunk(spectra, tm_size)
     half = own_block.shape[2] // 2
     norm_scale = 1.0 / half
@@ -88,11 +89,12 @@
 
     other_mask = jnp.where(partner_mask[0] == all_bits, partner_mask[1], partner_mask[0])
     branches = [exchange(m) for m in range(1, all_bits)]
-    full_partner, other_partner = lax.switch(
-        jnp.clip(other_mask - 1, 0, all_bits - 2), branches, own_block
+    full_spectra, other_spectra = lax.switch(
+        jnp.clip(other_mask - 1, 0, all_bits - 2), branches, spectra
     )
-    full_term = column_terms(full_partner)
-    other_term = column_terms(other_partner)
+    partners = by_channel_chunk(jnp.concatenate([full_spectra, other_spectra], axis=0), tm_size)
+    full_term = column_terms(partners[:, :in_dev])
+    other_term = column_terms(partners[:, in_dev:])
     pair_terms = [column_terms(own_block)]
     for round_index in range(ROUNDS):
         is_full = partner_mask[round_index] == all_bits

time: 87.1 us -> 112 us (1.29)
  the two profiles are of different devices: /device:TPU:88 before, /device:TPU:4 now
where the time goes in v4:
time: 112 us
  waiting for transfers between devices  47 us (42%)
  starting transfers between devices  43.2 us (39%)
  local copies, waits for them, and re-layouts  8.69 us (8%)
  other arithmetic  5.28 us (5%)
  matrix products  4.94 us (4%)
  between operations  2.61 us (2%)
    all_to_all x2, waiting for transfers between devices, by_channel_chunk(): got = lax.all_to_all(send, 'tm', 0, 0, tiled=True)  26.8 us
    all_to_all x2, starting transfers between devices, by_channel_chunk(): got = lax.all_to_all(send, 'tm', 0, 0, tiled=True)  19.5 us
    ppermute x1, waiting for transfers between devices, both(): other = lax.ppermute(x, 'inp', [(i, i ^ m) for i in range(inp_size)])  14.4 us
    ppermute x1, starting transfers between devices, both(): other = lax.ppermute(x, 'inp', [(i, i ^ m) for i in range(inp_size)])  12.1 us
    ppermute x1, starting transfers between devices, both(): full = lax.ppermute(x, 'inp', [(i, i ^ all_bits) for i in range(inp_size)])  9.89 us
    ppermute x1, waiting for transfers between devices, both(): full = lax.ppermute(x, 'inp', [(i, i ^ all_bits) for i in range(inp_size)])  5.74 us
    dot_general x1, matrix products, channelize(): jnp.dot(filtered.reshape(in_dev * spec_dev, n_fft), dft_table, precision=...  2.74 us
    another operation x3, local copies, waits for them, and re-layouts, on_device(): return jnp.stack(pair_terms, axis=1)  2.53 us
  transfers between devices with their start and end apart: 5, of which 3 were waited for; matrix products, arithmetic and copies ran while one was open for 7% of the time, Pallas kernels for 0%

profile of v4, /device:TPU:4, one launch (start us, length us, event | category | flops | bytes accessed | tf_op | source)
XLA Modules:
  0.0 112.0 jit_solution(9069050164828682824)
XLA Ops:
  0.0 1.0 slice.46
  1.0 1.7 %collective-permute-start.124 = (bf16[16,3,1024]{2,1,0:T(4,128)(2,1)S(1)}, bf16[16,3,1024]{2,1,0:T(4,128)(2,1)S(1)}, u32[]{:S(2)}, u32[]{:S(2)}) collective-permute-start(bf16[16,3,1024]{2,1,0:T(4,128)(2,1)S(1)} %slice.46), channel_id=1, source_target_pairs={{0,1},{1,2},{2,3},{3,4},{4,5},{5,6},{6,7},{8,9},{9,10},{10,11},{11... | collective-permute-start | bytes 294920 | tf_op jit(solution)/shard_map/ppermute | solution.py:15
  3.4 0.6 multiply_subtract_fusion
  4.4 2.7 %fusion.5 = bf16[128,1024]{1,0:T(8,128)(2,1)S(1)} fusion(f32[1024,512]{1,0:T(8,128)S(1)} %bitcast.112, f32[1024,512]{1,0:T(8,128)S(1)} %bitcast.111, bf16[16,8,1024]{2,1,0:T(8,128)(2,1)S(1)} %copy-done, bf16[16,3,1024]{2,1,0:T(4,128)(2,1)S(1)} %collective-permute-done.124, f32[1024]{0:T(1024)S(1)} %bitcast.116, f32[1024]{0:T(1024)S(1)} %bitcast.117, ...), kind=kOutput, calls=%fused_computation.10 | convolution fusion | flops 1614413824 | bytes 4833280 | tf_op jit(solution)/shard_map/dot_general | solution.py:45
  7.2 0.9 pad_maximum_fusion.1
  8.0 13.4 %all-to-all-start = ((bf16[8,16,8,2,128]{4,2,3,1,0:T(8,128)(2,1)}), bf16[8,16,8,2,128]{4,2,3,1,0:T(8,128)(2,1)S(1)}, u32[]{:S(2)}, u32[]{:S(2)}) async-start(bf16[8,16,8,2,128]{4,2,3,1,0:T(8,128)(2,1)} %pad_maximum_fusion.1), calls=%async_computation | async-start | bytes 1048576 | tf_op jit(solution)/shard_map/all_to_all | solution.py:61
  21.5 0.6 fusion.50
  23.8 42.7 %conditional.1 = (bf16[16,8,2,512]{3,2,1,0:T(2,128)(2,1)}, bf16[16,8,2,512]{3,2,1,0:T(2,128)(2,1)}) conditional(s32[]{:T(128)} %clamp.3, bf16[16,8,2,512]{3,1,2,0:T(8,128)(2,1)S(1)} %bitcast.74, bf16[16,8,2,512]{3,1,2,0:T(8,128)(2,1)S(1)} %bitcast.106, bf16[16,8,2,512]{3,1,2,0:T(8,128)(2,1)S(1)} %bitcast.47, ...), branch_computations={%region_0.1_spmd, %region_1.2_spmd, %region_2.3_spmd, %region_3.4_... | conditional | bytes 2621536 | solution.py:92
  24.4 9.9 %collective-permute-start.94 = (bf16[16,8,2,512]{3,2,1,0:T(2,128)(2,1)S(1)}, bf16[16,8,2,512]{3,2,1,0:T(2,128)(2,1)}, u32[]{:S(2)}, u32[]{:S(2)}) collective-permute-start(bf16[16,8,2,512]{3,2,1,0:T(2,128)(2,1)S(1)} %copy.260), channel_id=1, source_target_pairs={{0,504},{8,496},{16,488},{24,480},{32,472},{40,464},{48,456},{56,4... | collective-permute-start | bytes 786440 | tf_op jit(solution)/shard_map/cond/branch_47_fun/ppermute | solution.py:85
  34.3 12.1 %collective-permute-start.95 = (bf16[16,8,2,512]{3,2,1,0:T(2,128)(2,1)S(1)}, bf16[16,8,2,512]{3,2,1,0:T(2,128)(2,1)}, u32[]{:S(2)}, u32[]{:S(2)}) collective-permute-start(bf16[16,8,2,512]{3,2,1,0:T(2,128)(2,1)S(1)} %copy.260), channel_id=1, source_target_pairs={{0,384},{8,392},{16,400},{24,408},{32,416},{40,424},{48,432},{56,4... | collective-permute-start | bytes 786440 | tf_op jit(solution)/shard_map/cond/branch_47_fun/ppermute | solution.py:86
  46.4 5.7 %collective-permute-done.94 = bf16[16,8,2,512]{3,2,1,0:T(2,128)(2,1)} collective-permute-done((bf16[16,8,2,512]{3,2,1,0:T(2,128)(2,1)S(1)}, bf16[16,8,2,512]{3,2,1,0:T(2,128)(2,1)}, u32[]{:S(2)}, u32[]{:S(2)}) %collective-permute-start.94) | collective-permute-done | bytes 262176 | tf_op jit(solution)/shard_map/cond/branch_47_fun/ppermute | solution.py:85
  52.1 14.4 %collective-permute-done.95 = bf16[16,8,2,512]{3,2,1,0:T(2,128)(2,1)} collective-permute-done((bf16[16,8,2,512]{3,2,1,0:T(2,128)(2,1)S(1)}, bf16[16,8,2,512]{3,2,1,0:T(2,128)(2,1)}, u32[]{:S(2)}, u32[]{:S(2)}) %collective-permute-start.95) | collective-permute-done | bytes 262176 | tf_op jit(solution)/shard_map/cond/branch_47_fun/ppermute | solution.py:86
  66.5 1.7 %pad_maximum_fusion.2 = bf16[32,8,2,512]{3,2,1,0:T(2,128)(2,1)S(1)} fusion(bf16[16,8,2,512]{3,2,1,0:T(2,128)(2,1)} %get-tuple-element.70, bf16[16,8,2,512]{3,2,1,0:T(2,128)(2,1)} %get-tuple-element.69), kind=kLoop, calls=%fused_computation.20 | loop fusion | flops 262144 | bytes 1048576 | tf_op jit(solution)/shard_map/concatenate | solution.py:95
  68.8 0.5 pad_maximum_fusion
  69.3 1.1 %copy.276 = bf16[8,32,8,2,128]{4,2,3,1,0:T(8,128)(2,1)} copy(bf16[8,32,8,2,128]{4,0,2,3,1:T(8,128)(2,1)S(1)} %pad_maximum_fusion) | data formatting | bytes 2097152 | tf_op jit(solution)/shard_map/concatenate | solution.py:60
  70.4 6.0 %all-to-all-start.1 = ((bf16[8,32,8,2,128]{4,2,3,1,0:T(8,128)(2,1)}), bf16[8,32,8,2,128]{4,2,3,1,0:T(8,128)(2,1)S(1)}, u32[]{:S(2)}, u32[]{:S(2)}) async-start(bf16[8,32,8,2,128]{4,2,3,1,0:T(8,128)(2,1)} %copy.276), calls=%async_computation.1 | async-start | bytes 2097152 | tf_op jit(solution)/shard_map/all_to_all | solution.py:61
  77.3 0.4 copy.211
  78.8 0.4 copy.282
  79.2 26.8 %all-to-all-done.1 = bf16[8,32,8,2,128]{4,2,3,1,0:T(8,128)(2,1)S(1)} async-done(((bf16[8,32,8,2,128]{4,2,3,1,0:T(8,128)(2,1)}), bf16[8,32,8,2,128]{4,2,3,1,0:T(8,128)(2,1)S(1)}, u32[]{:S(2)}, u32[]{:S(2)}) %all-to-all-start.1) | async-done | bytes 1048608 | tf_op jit(solution)/shard_map/all_to_all | solution.py:61
  106.5 0.4 copy.287
  107.8 1.4 %select_bitcast_fusion.1 = (f32[16,1,16,128]{0,2,3,1:T(8,128)}, f32[16,1,16,128]{0,2,3,1:T(8,128)S(1)}) fusion(f32[128,16,16]{2,1,0:T(8,128)S(1)} %convolution_multiply_fusion, pred[]{:T(512)S(6)} %eq.10, pred[]{:T(512)S(6)} %eq.11, bf16[128,16,128]{2,1,0:T(8,128)(2,1)S(1)} %copy.286, bf16[128,16,128]{2,1,0:T(8,128)(2,1)S(1)} %copy.212), kind=kOutput, calls=%fused_computation.13 | convolution fusion | flops 8486912 | bytes 1441794 | tf_op jit(solution)/shard_map/cix,cjx->ijc/dot_general | solution.py:80
  109.1 1.6 %copy.283 = f32[16,1,16,128]{3,2,1,0:T(8,128)S(1)} copy(f32[16,1,16,128]{0,2,3,1:T(8,128)} %get-tuple-element.71) | data formatting | bytes 262144 | tf_op jit(solution)/shard_map/stack | solution.py:102
  110.8 0.4 copy.284
  111.2 0.8 pad_maximum_fusion.3
  (25 shorter events, 4.2 us)
Async XLA Ops:
  1.0 3.1 %collective-permute-start.124 = (bf16[16,3,1024]{2,1,0:T(4,128)(2,1)S(1)}, bf16[16,3,1024]{2,1,0:T(4,128)(2,1)S(1)}, u32[]{:S(2)}, u32[]{:S(2)}) collective-permute-start(bf16[16,3,1024]{2,1,0:T(4,128)(2,1)S(1)} %slice.46), channel_id=1, source_target_pairs={{0,1},{1,2},{2,3},{3,4},{4,5},{5,6},{6,7},{8,9},{9,10},{10,11},{11... | collective-permute-start | bytes 294920 | tf_op jit(solution)/shard_map/ppermute | solution.py:15
  3.4 0.7 copy-start.1
  3.4 1.0 copy-start
  7.1 14.4 %copy-start.2 = (s32[2]{0:T(128)S(1)}, s32[2]{0:T(128)}, u32[]{:S(2)}) copy-start(s32[2]{0:T(128)} %param.67) | copy-start | bytes 28
  8.0 62.4 %all-to-all-start = ((bf16[8,16,8,2,128]{4,2,3,1,0:T(8,128)(2,1)}), bf16[8,16,8,2,128]{4,2,3,1,0:T(8,128)(2,1)S(1)}, u32[]{:S(2)}, u32[]{:S(2)}) async-start(bf16[8,16,8,2,128]{4,2,3,1,0:T(8,128)(2,1)} %pad_maximum_fusion.1), calls=%async_computation | async-start | bytes 1048576 | tf_op jit(solution)/shard_map/all_to_all | solution.py:61
  24.4 27.7 %collective-permute-start.94 = (bf16[16,8,2,512]{3,2,1,0:T(2,128)(2,1)S(1)}, bf16[16,8,2,512]{3,2,1,0:T(2,128)(2,1)}, u32[]{:S(2)}, u32[]{:S(2)}) collective-permute-start(bf16[16,8,2,512]{3,2,1,0:T(2,128)(2,1)S(1)} %copy.260), channel_id=1, source_target_pairs={{0,504},{8,496},{16,488},{24,480},{32,472},{40,464},{48,456},{56,4... | collective-permute-start | bytes 786440 | tf_op jit(solution)/shard_map/cond/branch_47_fun/ppermute | solution.py:85
  34.3 32.3 %collective-permute-start.95 = (bf16[16,8,2,512]{3,2,1,0:T(2,128)(2,1)S(1)}, bf16[16,8,2,512]{3,2,1,0:T(2,128)(2,1)}, u32[]{:S(2)}, u32[]{:S(2)}) collective-permute-start(bf16[16,8,2,512]{3,2,1,0:T(2,128)(2,1)S(1)} %copy.260), channel_id=1, source_target_pairs={{0,384},{8,392},{16,400},{24,408},{32,416},{40,424},{48,432},{56,4... | collective-permute-start | bytes 786440 | tf_op jit(solution)/shard_map/cond/branch_47_fun/ppermute | solution.py:86
  70.4 35.6 %all-to-all-start.1 = ((bf16[8,32,8,2,128]{4,2,3,1,0:T(8,128)(2,1)}), bf16[8,32,8,2,128]{4,2,3,1,0:T(8,128)(2,1)S(1)}, u32[]{:S(2)}, u32[]{:S(2)}) async-start(bf16[8,32,8,2,128]{4,2,3,1,0:T(8,128)(2,1)} %copy.276), calls=%async_computation.1 | async-start | bytes 2097152 | tf_op jit(solution)/shard_map/all_to_all | solution.py:61

commit v5 on v2

--- a/solution.py
+++ b/solution.py
@@ -91,13 +91,12 @@
     full_partner, other_partner = lax.switch(
         jnp.clip(other_mask - 1, 0, all_bits - 2), branches, own_block
     )
-    full_term = column_terms(full_partner)
-    other_term = column_terms(other_partner)
-    pair_terms = [column_terms(own_block)]
+    blocks = [own_block]
     for round_index in range(ROUNDS):
         is_full = partner_mask[round_index] == all_bits
-        pair_terms.append(jnp.where(is_full, full_term, other_term))
-    return jnp.stack(pair_terms, axis=1)
+        blocks.append(jnp.where(is_full, full_partner, other_partner))
+    terms = column_terms(jnp.concatenate(blocks, axis=1))
+    return terms.reshape(terms.shape[0], ROUNDS + 1, -1, terms.shape[2])
 
 
 def solution(mesh):

time: 87.1 us -> 90.9 us (1.044)
  the two profiles are of different devices: /device:TPU:88 before, /device:TPU:18 now
where the time goes in v5:
time: 90.9 us; the launch traced here: 90.5 us
  waiting for transfers between devices  48.2 us (53%)
  starting transfers between devices  28.3 us (31%)
  local copies, waits for them, and re-layouts  3.95 us (4%)
  matrix products  3.68 us (4%)
  other arithmetic  3.57 us (4%)
  between operations  2.81 us (3%)
    ppermute x1, waiting for transfers between devices, both(): other = lax.ppermute(x, 'inp', [(i, i ^ m) for i in range(inp_size)])  16.8 us
    ppermute x1, waiting for transfers between devices, both(): full = lax.ppermute(x, 'inp', [(i, i ^ all_bits) for i in range(inp_size)])  14.9 us
    all_to_all x1, waiting for transfers between devices, by_channel_chunk(): got = lax.all_to_all(send, 'tm', 0, 0, tiled=True)  12.5 us
    all_to_all x1, starting transfers between devices, by_channel_chunk(): got = lax.all_to_all(send, 'tm', 0, 0, tiled=True)  9.85 us
    ppermute x1, starting transfers between devices, both(): other = lax.ppermute(x, 'inp', [(i, i ^ m) for i in range(inp_size)])  8.38 us
    ppermute x1, starting transfers between devices, both(): full = lax.ppermute(x, 'inp', [(i, i ^ all_bits) for i in range(inp_size)])  8.1 us
    ppermute x1, waiting for transfers between devices, shifted(): return lax.ppermute(block, axis, route)  3.99 us
    dot_general x1, matrix products, channelize(): jnp.dot(filtered.reshape(in_dev * spec_dev, n_fft), dft_table, precision=...  2.74 us
  transfers between devices with their start and end apart: 4, of which 4 were waited for; matrix products, arithmetic and copies ran while one was open for 2% of the time, Pallas kernels for 0%

profile of v5, /device:TPU:18, one launch (start us, length us, event | category | flops | bytes accessed | tf_op | source)
XLA Modules:
  0.0 90.5 jit_solution(7643266811519101015)
XLA Ops:
  0.0 1.0 %slice.40 = bf16[16,3,1024]{2,1,0:T(4,128)(2,1)S(1)} slice(bf16[16,8,1024]{2,1,0:T(8,128)(2,1)} %param.65), slice={[0:16], [5:8], [0:1024]} | slice | bytes 196608 | tf_op jit(solution)/shard_map/slice | solution.py:37
  1.0 1.9 %collective-permute-start.124 = (bf16[16,3,1024]{2,1,0:T(4,128)(2,1)S(1)}, bf16[16,3,1024]{2,1,0:T(4,128)(2,1)S(1)}, u32[]{:S(2)}, u32[]{:S(2)}) collective-permute-start(bf16[16,3,1024]{2,1,0:T(4,128)(2,1)S(1)} %slice.40), channel_id=1, source_target_pairs={{0,1},{1,2},{2,3},{3,4},{4,5},{5,6},{6,7},{8,9},{9,10},{10,11},{11... | collective-permute-start | bytes 294920 | tf_op jit(solution)/shard_map/ppermute | solution.py:15
  3.0 0.3 fusion.52
  3.2 0.3 fusion.55
  3.6 0.6 multiply_subtract_fusion
  4.2 0.1 copy-done.1
  4.3 4.0 %collective-permute-done.124 = bf16[16,3,1024]{2,1,0:T(4,128)(2,1)S(1)} collective-permute-done((bf16[16,3,1024]{2,1,0:T(4,128)(2,1)S(1)}, bf16[16,3,1024]{2,1,0:T(4,128)(2,1)S(1)}, u32[]{:S(2)}, u32[]{:S(2)}) %collective-permute-start.124) | collective-permute-done | bytes 98336 | tf_op jit(solution)/shard_map/ppermute | solution.py:15
  8.3 2.7 %fusion.16 = bf16[128,1024]{1,0:T(8,128)(2,1)S(1)} fusion(f32[1024,512]{1,0:T(8,128)S(1)} %bitcast.26, f32[1024,512]{1,0:T(8,128)S(1)} %bitcast.25, bf16[16,8,1024]{2,1,0:T(8,128)(2,1)S(1)} %copy-done, bf16[16,3,1024]{2,1,0:T(4,128)(2,1)S(1)} %collective-permute-done.124, f32[1024]{0:T(1024)S(1)} %bitcast.31, f32[1024]{0:T(1024)S(1)} %bitcast.32, ...), kind=kOutput, calls=%fused_computation.14 | convolution fusion | flops 1614413824 | bytes 4833280 | tf_op jit(solution)/shard_map/dot_general | solution.py:45
  11.1 0.8 pad_maximum_fusion
  12.0 9.9 %all-to-all-start = ((bf16[8,16,8,2,128]{4,2,3,1,0:T(8,128)(2,1)}), bf16[8,16,8,2,128]{4,2,3,1,0:T(8,128)(2,1)S(1)}, u32[]{:S(2)}, u32[]{:S(2)}) async-start(bf16[8,16,8,2,128]{4,2,3,1,0:T(8,128)(2,1)} %pad_maximum_fusion), calls=%async_computation | async-start | bytes 1048576 | tf_op jit(solution)/shard_map/all_to_all | solution.py:61
  21.8 0.6 fusion.61
  25.1 12.5 %all-to-all-done = bf16[8,16,8,2,128]{4,2,3,1,0:T(8,128)(2,1)S(1)} async-done(((bf16[8,16,8,2,128]{4,2,3,1,0:T(8,128)(2,1)}), bf16[8,16,8,2,128]{4,2,3,1,0:T(8,128)(2,1)S(1)}, u32[]{:S(2)}, u32[]{:S(2)}) %all-to-all-start) | async-done | bytes 524320 | tf_op jit(solution)/shard_map/all_to_all | solution.py:61
  37.6 0.1 copy.72
  37.8 0.4 copy.135
  38.3 0.2 maximum_select_fusion
  38.5 0.4 copy.136
  38.9 48.2 %conditional.1 = (bf16[128,16,128]{2,1,0:T(8,128)(2,1)}, bf16[128,16,128]{2,1,0:T(8,128)(2,1)}) conditional(s32[]{:T(128)} %clamp.3, bf16[128,16,128]{2,1,0:T(8,128)(2,1)S(1)} %copy.135, bf16[128,16,128]{2,1,0:T(8,128)(2,1)S(1)} %copy.135, bf16[128,16,128]{2,1,0:T(8,128)(2,1)S(1)} %copy.135, ...), branch_computations={%region_0.1_spmd, %region_1.2_spmd, %region_2.3_spmd, %region_3.4_... | conditional | bytes 4194400 | solution.py:91
  38.9 8.1 %collective-permute-start.64 = (bf16[128,16,128]{2,1,0:T(8,128)(2,1)S(1)}, bf16[128,16,128]{2,1,0:T(8,128)(2,1)}, u32[]{:S(2)}, u32[]{:S(2)}) collective-permute-start(bf16[128,16,128]{2,1,0:T(8,128)(2,1)S(1)} %param.32), channel_id=1, source_target_pairs={{0,504},{8,496},{16,488},{24,480},{32,472},{40,464},{48,456},{56,4... | collective-permute-start | bytes 1572872 | tf_op jit(solution)/shard_map/cond/branch_32_fun/ppermute | solution.py:84
  47.0 8.4 %collective-permute-start.65 = (bf16[128,16,128]{2,1,0:T(8,128)(2,1)S(1)}, bf16[128,16,128]{2,1,0:T(8,128)(2,1)}, u32[]{:S(2)}, u32[]{:S(2)}) collective-permute-start(bf16[128,16,128]{2,1,0:T(8,128)(2,1)S(1)} %param.32), channel_id=1, source_target_pairs={{0,264},{8,256},{16,280},{24,272},{32,296},{40,288},{48,312},{56,3... | collective-permute-start | bytes 1572872 | tf_op jit(solution)/shard_map/cond/branch_32_fun/ppermute | solution.py:85
  55.4 14.9 %collective-permute-done.64 = bf16[128,16,128]{2,1,0:T(8,128)(2,1)} collective-permute-done((bf16[128,16,128]{2,1,0:T(8,128)(2,1)S(1)}, bf16[128,16,128]{2,1,0:T(8,128)(2,1)}, u32[]{:S(2)}, u32[]{:S(2)}) %collective-permute-start.64) | collective-permute-done | bytes 524320 | tf_op jit(solution)/shard_map/cond/branch_32_fun/ppermute | solution.py:84
  70.3 16.8 %collective-permute-done.65 = bf16[128,16,128]{2,1,0:T(8,128)(2,1)} collective-permute-done((bf16[128,16,128]{2,1,0:T(8,128)(2,1)S(1)}, bf16[128,16,128]{2,1,0:T(8,128)(2,1)}, u32[]{:S(2)}, u32[]{:S(2)}) %collective-permute-start.65) | collective-permute-done | bytes 524320 | tf_op jit(solution)/shard_map/cond/branch_32_fun/ppermute | solution.py:85
  87.1 1.3 %broadcast_select_fusion.1 = (bf16[128,16,128]{2,1,0:T(8,128)(2,1)S(1)}, bf16[128,16,128]{2,1,0:T(8,128)(2,1)S(1)}) fusion(bf16[128,16,128]{2,1,0:T(8,128)(2,1)} %get-tuple-element.69, bf16[128,16,128]{2,1,0:T(8,128)(2,1)} %get-tuple-element.70, pred[]{:T(512)S(6)} %eq.10, pred[]{:T(512)S(6)} %eq.11), kind=kLoop, calls=%fused_computation.34 | loop fusion | flops 524288 | bytes 2097154 | tf_op jit(solution)/shard_map/jit(_where)/select_n | solution.py:97
  88.4 0.9 %fusion.13 = f32[16,48,128]{1,0,2:T(8,128)S(1)} fusion(bf16[128,16,128]{2,1,0:T(8,128)(2,1)S(1)} %copy.136, bf16[128,16,128]{2,1,0:T(8,128)(2,1)S(1)} %get-tuple-element.72, bf16[128,16,128]{2,1,0:T(8,128)(2,1)S(1)} %get-tuple-element.71, bf16[128,16,128]{2,1,0:T(8,128)(2,1)S(1)} %copy.135), kind=kOutput, calls=%fused_computation.13 | convolution fusion | flops 29982720 | bytes 2490368 | tf_op jit(solution)/shard_map/cix,cjx->ijc/dot_general | solution.py:79
  89.3 1.2 %copy.137 = f32[16,48,128]{2,1,0:T(8,128)} copy(f32[16,48,128]{1,0,2:T(8,128)S(1)} %fusion.13) | data formatting | bytes 786432 | tf_op jit(solution)/shard_map/mul | solution.py:80
  (9 shorter events, 0.1 us)
Async XLA Ops:
  1.0 7.3 %collective-permute-start.124 = (bf16[16,3,1024]{2,1,0:T(4,128)(2,1)S(1)}, bf16[16,3,1024]{2,1,0:T(4,128)(2,1)S(1)}, u32[]{:S(2)}, u32[]{:S(2)}) collective-permute-start(bf16[16,3,1024]{2,1,0:T(4,128)(2,1)S(1)} %slice.40), channel_id=1, source_target_pairs={{0,1},{1,2},{2,3},{3,4},{4,5},{5,6},{6,7},{8,9},{9,10},{10,11},{11... | collective-permute-start | bytes 294920 | tf_op jit(solution)/shard_map/ppermute | solution.py:15
  3.6 0.7 copy-start.1
  3.6 4.7 %copy-start = (bf16[16,8,1024]{2,1,0:T(8,128)(2,1)S(1)}, bf16[16,8,1024]{2,1,0:T(8,128)(2,1)}, u32[]{:S(2)}) copy-start(bf16[16,8,1024]{2,1,0:T(8,128)(2,1)} %param.65) | copy-start | bytes 786436
  11.1 10.8 %copy-start.2 = (s32[2]{0:T(128)S(1)}, s32[2]{0:T(128)}, u32[]{:S(2)}) copy-start(s32[2]{0:T(128)} %param.67) | copy-start | bytes 28
  12.0 25.7 %all-to-all-start = ((bf16[8,16,8,2,128]{4,2,3,1,0:T(8,128)(2,1)}), bf16[8,16,8,2,128]{4,2,3,1,0:T(8,128)(2,1)S(1)}, u32[]{:S(2)}, u32[]{:S(2)}) async-start(bf16[8,16,8,2,128]{4,2,3,1,0:T(8,128)(2,1)} %pad_maximum_fusion), calls=%async_computation | async-start | bytes 1048576 | tf_op jit(solution)/shard_map/all_to_all | solution.py:61
  38.9 31.4 %collective-permute-start.64 = (bf16[128,16,128]{2,1,0:T(8,128)(2,1)S(1)}, bf16[128,16,128]{2,1,0:T(8,128)(2,1)}, u32[]{:S(2)}, u32[]{:S(2)}) collective-permute-start(bf16[128,16,128]{2,1,0:T(8,128)(2,1)S(1)} %param.32), channel_id=1, source_target_pairs={{0,504},{8,496},{16,488},{24,480},{32,472},{40,464},{48,456},{56,4... | collective-permute-start | bytes 1572872 | tf_op jit(solution)/shard_map/cond/branch_32_fun/ppermute | solution.py:84
  47.0 40.1 %collective-permute-start.65 = (bf16[128,16,128]{2,1,0:T(8,128)(2,1)S(1)}, bf16[128,16,128]{2,1,0:T(8,128)(2,1)}, u32[]{:S(2)}, u32[]{:S(2)}) collective-permute-start(bf16[128,16,128]{2,1,0:T(8,128)(2,1)S(1)} %param.32), channel_id=1, source_target_pairs={{0,264},{8,256},{16,280},{24,272},{32,296},{40,288},{48,312},{56,3... | collective-permute-start | bytes 1572872 | tf_op jit(solution)/shard_map/cond/branch_32_fun/ppermute | solution.py:85
